TPU v7x, 32 devices: a whole 2x2x4 slice. The times are simulated.
32 devices in a mesh: stn: 16 (over z, x, core), chan: 2 (over y).
Axes of the slice: x: 2, y: 2, z: 4, core: 2. Of those that a mesh axis runs over, the one named last changes fastest.
Arguments:
- screen: float32 [32, 512, 512], P('stn'), may hold values from -6 to 6
- pierce_coords: float32 [2, 16, 2, 16, 1024], P(None, 'stn', 'chan'), may hold values from 0 to 1
- query_dest: int32 [16, 2, 16, 1024], P('stn', 'chan'), may hold values from 0 to 4096, as said below
- positions: float32 [3, 256], P(None, 'stn'), may hold values from -50 to 50
- directions: float32 [3, 512], replicated, may hold values from -0.7 to 0.7
- freq_ratio: float32 [64], P('chan'), may hold values from 0.7 to 1.4
- source_flux: float32 [512], replicated, may hold values from 0.2 to 5
- spectral_index: float32 [512], replicated, may hold values from -1.5 to 0.5
Outputs:
- visibilities: float32 [64, 2, 256, 256], P('chan', None, 'stn')
Inputs may be any that keep to these rules, and one draw needn't show every extreme that they name: `query_dest`: in each block every number 0 to 4095 appears in exactly one slot and empty slots hold 4096; an owner's live slots come first in its row; one owner, the same for every block, has all 1024 of its slots live in every block.
All inputs are finite; a program needn't handle non-finite values.
Results may differ from a plain program's by a relative error of at most 0.008.
Values may be sent and summed in bfloat16 or wider, within the bound.
No kernel may reach another device: no remote copies, remote signals or barrier semaphores. Data moves between devices by JAX's collectives and lax.ppermute only.
A program may use at most 128 MiB of HBM per device.

v0:
```python
import math
import jax
import jax.numpy as jnp
from jax import lax
from jax.sharding import PartitionSpec as P

TWO_PI = 2.0 * math.pi


def interpolate(values, coords, strip_rows, tile_cols):
    row_pos = coords[0] * (strip_rows - 1)
    col_pos = coords[1] * (tile_cols - 1)
    row_low = jnp.clip(jnp.floor(row_pos), 0.0, strip_rows - 2.0)
    col_low = jnp.clip(jnp.floor(col_pos), 0.0, tile_cols - 2.0)
    frac_y = row_pos - row_low
    frac_x = col_pos - col_low
    corner = row_low.astype(jnp.int32) * tile_cols + col_low.astype(jnp.int32)
    lower_pair = (1.0 - frac_x) * values[corner] + frac_x * values[corner + 1]
    upper_pair = (1.0 - frac_x) * values[corner + tile_cols] + frac_x * values[
        corner + tile_cols + 1
    ]
    return (1.0 - frac_y) * lower_pair + frac_y * upper_pair


def make_phasors(station_rows, iono_rows, directions, freq_ratio):
    delays = (
        station_rows[:, 0:1] * directions[0][None, :]
        + station_rows[:, 1:2] * directions[1][None, :]
    )
    delays = delays + station_rows[:, 2:3] * directions[2][None, :]
    angles = (TWO_PI * freq_ratio)[None, :, None] * delays[:, None, :] + iono_rows[
        :, None, :
    ] / freq_ratio[None, :, None]
    return jnp.concatenate([jnp.cos(angles), jnp.sin(angles)], axis=-1).astype(jnp.bfloat16)


def spectrum(source_flux, spectral_index, freq_ratio, count):
    return (
        source_flux[None, :]
        * jnp.exp(spectral_index[None, :] * jnp.log(freq_ratio)[:, None])
        / math.sqrt(count)
    )


def weight_rows(phasors, intensity):
    sources = intensity.shape[1]
    real_part = (phasors[:, :, :sources].astype(jnp.float32) * intensity[None]).astype(jnp.bfloat16)
    imag_part = (phasors[:, :, sources:].astype(jnp.float32) * intensity[None]).astype(jnp.bfloat16)
    upper_rows = jnp.concatenate([real_part, imag_part], axis=-1)
    lower_rows = jnp.concatenate([imag_part, -real_part], axis=-1)
    return jnp.concatenate([upper_rows, lower_rows], axis=0)


def body(
    screen,
    pierce_coords,
    query_dest,
    positions,
    directions,
    freq_ratio,
    source_flux,
    spectral_index,
):
    groups = lax.axis_size("stn")
    tile_cols = screen.shape[2]
    strip_rows = screen.shape[0] * screen.shape[1]
    values = screen.reshape(-1)
    capacity = query_dest.shape[3]
    coords = pierce_coords.reshape(2, groups, capacity)
    sampled = interpolate(
        values,
        lax.all_to_all(coords, "stn", split_axis=1, concat_axis=1, tiled=True),
        strip_rows,
        tile_cols,
    )
    returned = lax.all_to_all(sampled, "stn", split_axis=0, concat_axis=0, tiled=True)
    stations_local = positions.shape[1]
    local_sources = source_flux.shape[0] // lax.axis_size("chan")
    queries = stations_local * local_sources
    buffer = (
        jnp.zeros((queries + 1,), jnp.float32).at[query_dest.reshape(-1)].set(returned.reshape(-1))
    )
    own_iono = buffer[:queries].reshape(stations_local, local_sources)
    iono_phase = lax.all_gather(own_iono, "chan", axis=1, tiled=True)
    station_rows = positions.T
    own_phasors = make_phasors(station_rows, iono_phase, directions, freq_ratio)
    intensity = spectrum(source_flux, spectral_index, freq_ratio, source_flux.shape[0])
    weighted = weight_rows(own_phasors, intensity)
    total_stations = stations_local * groups
    channels = freq_ratio.shape[0]
    columns = jnp.einsum(
        "ack,nck->can",
        weighted,
        make_phasors(
            lax.all_gather(station_rows, "stn", axis=0, tiled=True),
            lax.all_gather(iono_phase, "stn", axis=0, tiled=True),
            directions,
            freq_ratio,
        ),
        preferred_element_type=jnp.float32,
    )
    visible = columns.reshape(channels, 2, stations_local, total_stations)
    first_row = lax.axis_index("stn") * stations_local
    rows_global = first_row + jnp.arange(stations_local, dtype=jnp.int32)
    cross_only = rows_global[:, None] != jnp.arange(total_stations, dtype=jnp.int32)[None, :]
    return jnp.where(cross_only[None, None], visible, jnp.zeros_like(visible))


def solution(mesh):
    in_specs = (
        P("stn", None, None),
        P(None, "stn", "chan", None, None),
        P("stn", "chan", None, None),
        P(None, "stn"),
        P(),
        P("chan"),
        P(),
        P(),
    )
    out_specs = P("chan", None, "stn", None)
    return jax.shard_map(body, mesh=mesh, in_specs=in_specs, out_specs=out_specs, check_vma=False)
```

profile of v0, /device:TPU:0, one launch (start us, length us, event | category | flops | bytes accessed | tf_op | source)
XLA Modules:
  0.0 576.7 jit_solution(3012017053386605129)
XLA Ops:
  0.0 1.7 copy.15
  1.7 7.4 %all-to-all-start = ((f32[2,16,1024]{2,0,1:T(2,128)}), f32[2,16,1024]{2,0,1:T(2,128)S(1)}, u32[]{:S(2)}, u32[]{:S(2)}) async-start(f32[2,16,1024]{2,0,1:T(2,128)} %bitcast.74), calls=%async_computation | async-start | bytes 262144 | tf_op jit(solution)/shard_map/all_to_all | solution.py:72
  9.1 0.9 copy.12
  10.0 0.1 compare_select_fusion.4
  10.0 0.8 fusion.17
  10.9 22.0 %all-gather = f32[16,16,3]{1,2,0:T(4,128)S(1)} all-gather(f32[1,16,3]{1,2,0:T(4,128)} %bitcast.98), channel_id=1, replica_groups=mesh['stn'=16,'chan'=2] {'stn'}, dimensions={0}, use_global_device_ids=true | all-gather | bytes 3264 | tf_op jit(solution)/shard_map/all_gather | solution.py:95
  32.9 0.1 reshape.551
  33.0 0.7 fusion.19
  33.6 0.8 slice_bitcast_fusion.2
  34.4 0.8 multiply_multiply_fusion
  35.2 0.1 multiply_add_fusion.3
  35.3 2.1 copy.13
  37.5 0.2 multiply_add_fusion
  37.6 0.0 all-to-all-done
  37.6 0.3 compare_select_fusion.3
  37.9 0.2 compare_select_fusion.2
  38.2 90.5 %gather_fusion.3 = f32[16384]{0:T(1024)S(1)} fusion(f32[524288]{0:T(1024)S(1)} %bitcast.75, s32[16384]{0:T(1024)S(1)} %broadcast_clamp_fusion), kind=kCustom, calls=%fused_computation.3 | custom fusion | bytes 196608 | tf_op jit(solution)/shard_map/gather | solution.py:19
  128.8 90.5 %gather_fusion.2 = f32[16384]{0:T(1024)S(1)} fusion(f32[524288]{0:T(1024)S(1)} %bitcast.76, s32[16384]{0:T(1024)S(1)} %broadcast_clamp_fusion.1), kind=kCustom, calls=%fused_computation.2 | custom fusion | bytes 196608 | tf_op jit(solution)/shard_map/gather | solution.py:19
  219.3 90.5 %gather_fusion.1 = f32[16384]{0:T(1024)S(1)} fusion(f32[524288]{0:T(1024)S(1)} %bitcast.77, s32[16384]{0:T(1024)S(1)} %broadcast_clamp_fusion.2), kind=kCustom, calls=%fused_computation.1 | custom fusion | bytes 196608 | tf_op jit(solution)/shard_map/gather | solution.py:18
  309.9 0.0 copy-start
  309.9 90.5 %gather_fusion = f32[16384]{0:T(1024)S(1)} fusion(f32[524288]{0:T(1024)S(1)} %bitcast.78, s32[16384]{0:T(1024)S(1)} %broadcast_clamp_fusion.3), kind=kCustom, calls=%fused_computation | custom fusion | bytes 196608 | tf_op jit(solution)/shard_map/gather | solution.py:18
  400.4 1.0 multiply_add_fusion.2
  401.4 3.5 all-to-all-start.1
  404.9 0.1 iota_compare_fusion
  405.0 6.8 %all-to-all-done.1 = f32[16,1,1024]{2,1,0:T(1,128)S(1)} async-done(((f32[16,1,1024]{2,1,0:T(1,128)}), f32[16,1,1024]{2,1,0:T(1,128)S(1)}, u32[]{:S(2)}, u32[]{:S(2)}) %all-to-all-start.1) | async-done | bytes 65568 | tf_op jit(solution)/shard_map/all_to_all | solution.py:76
  411.8 60.4 %scatter_custom_fusion = f32[4097]{0:T(1024)S(1)} fusion(s32[16384]{0:T(1024)S(1)} %bitcast.90, f32[16384]{0:T(1024)S(1)} %bitcast.91, f32[]{:T(128)} %constant.11.clone.1), kind=kCustom, calls=%fused_computation.55 | custom fusion | bytes 16392 | tf_op jit(solution)/shard_map/scatter | solution.py:81
  472.2 4.4 all_gather.9
  476.6 19.4 %all_gather.11 = f32[256,512]{1,0:T(8,128)S(1)} all-gather(f32[16,512]{1,0:T(8,128)S(1)} %all_gather.9), channel_id=1, replica_groups=mesh['stn'=16,'chan'=2] {'stn'}, dimensions={0}, use_global_device_ids=true | all-gather | bytes 557056 | tf_op jit(solution)/shard_map/all_gather | solution.py:96
  496.0 0.0 copy-done
  496.0 3.9 fusion.16
  499.9 4.3 multiply_convert_fusion.1
  504.2 62.5 %cosine_convert_fusion = (bf16[256,32,512]{2,0,1:T(8,128)(2,1)}, bf16[256,32,512]{2,0,1:T(8,128)(2,1)}) fusion(f32[32]{0:T(128)S(1)} %copy-done, f32[256,512]{1,0:T(8,128)S(1)} %all_gather.11, f32[256,512]{1,0:T(8,128)S(1)} %multiply_add_fusion, f32[32]{0:T(128)S(1)} %get-tuple-element.24), kind=kLoop, calls=%fused_computation.11 | loop fusion | flops 20971520 | bytes 17826048 | tf_op jit(solution)/shard_map/convert
  566.6 8.9 %fusion = f32[32,32,256]{2,1,0:T(8,128)S(1)} fusion(bf16[256,32,512]{2,0,1:T(8,128)(2,1)} %get-tuple-element.8, bf16[256,32,512]{2,0,1:T(8,128)(2,1)} %get-tuple-element.7, bf16[16,32,512]{2,0,1:T(8,128)(2,1)S(1)} %fusion.16, bf16[16,32,512]{2,0,1:T(8,128)(2,1)S(1)} %get-tuple-element.10, bf16[16,32,512]{2,0,1:T(8,128)(2,1)S(1)} %get-tuple-element.9), kind=kOutput, calls=%fused_computation.6 | convolution fusion | flops 578813952 | bytes 19398656 | tf_op jit(solution)/shard_map/ack,nck->can/dot_general | solution.py:91
  575.5 1.1 broadcast_select_fusion
  (9 shorter events, 0.1 us)
Async XLA Ops:
  1.7 36.0 %all-to-all-start = ((f32[2,16,1024]{2,0,1:T(2,128)}), f32[2,16,1024]{2,0,1:T(2,128)S(1)}, u32[]{:S(2)}, u32[]{:S(2)}) async-start(f32[2,16,1024]{2,0,1:T(2,128)} %bitcast.74), calls=%async_computation | async-start | bytes 262144 | tf_op jit(solution)/shard_map/all_to_all | solution.py:72
  309.9 186.1 %copy-start = (f32[32]{0:T(128)S(1)}, f32[32]{0:T(128)}, u32[]{:S(2)}) copy-start(f32[32]{0:T(128)} %param.13) | copy-start | bytes 388
  401.4 10.4 %all-to-all-start.1 = ((f32[16,1,1024]{2,1,0:T(1,128)}), f32[16,1,1024]{2,1,0:T(1,128)S(1)}, u32[]{:S(2)}, u32[]{:S(2)}) async-start(f32[16,1,1024]{2,1,0:T(1,128)} %multiply_add_fusion.2), calls=%async_computation.1 | async-start | bytes 131072 | tf_op jit(solution)/shard_map/all_to_all | solution.py:76
where the time goes:
time: 577 us
  local copies, waits for them, and re-layouts  429 us (74%)
  other arithmetic  75.1 us (13%)
  blocking collectives  45.8 us (8%)
  starting transfers between devices  10.9 us (2%)
  matrix products  8.92 us (2%)
  waiting for transfers between devices  6.79 us (1%)
    gather x2, local copies, waits for them, and re-layouts, interpolate(): lower_pair = (1.0 - frac_x) * values[corner] + frac_x * values[corner + 1]  181 us
    gather x1, local copies, waits for them, and re-layouts, interpolate(): values[corner + tile_cols + 1]  90.5 us
    gather x1, local copies, waits for them, and re-layouts, interpolate(): values[corner + tile_cols]  90.5 us
    another operation x1, other arithmetic  62.5 us
    scatter x1, local copies, waits for them, and re-layouts, body(): jnp.zeros((queries + 1,), jnp.float32).at[query_dest.reshape(-1)]  60.4 us
    all_gather x1, blocking collectives, body(): lax.all_gather(station_rows, 'stn', axis=0, tiled=True)  22 us
    all_gather x1, blocking collectives, body(): lax.all_gather(iono_phase, 'stn', axis=0, tiled=True)  19.4 us
  transfers between devices with their start and end apart: 2, of which 1 were waited for; matrix products, arithmetic and copies ran while one was open for 1% of the time, Pallas kernels for 0%

commit v1 on v0

--- a/solution.py
+++ b/solution.py
@@ -5,6 +5,22 @@
 from jax.sharding import PartitionSpec as P
 
 TWO_PI = 2.0 * math.pi
+
+
+def collect(x, axis, dim):
+    ways, here, step = (lax.axis_size(axis), lax.axis_index(axis), x.shape[dim])
+    shape = [n * ways if d == dim else n for d, n in enumerate(x.shape)]
+    full = lax.dynamic_update_slice_in_dim(jnp.zeros(shape, x.dtype), x, here * step, axis=dim)
+    going_up = going_down = x
+    for far in range(1, ways // 2 + 1):
+        going_up = lax.ppermute(going_up, axis, [(d, (d + 1) % ways) for d in range(ways)])
+        full = lax.dynamic_update_slice_in_dim(full, going_up, (here - far) % ways * step, axis=dim)
+        if 2 * far < ways:
+            going_down = lax.ppermute(going_down, axis, [(d, (d - 1) % ways) for d in range(ways)])
+            full = lax.dynamic_update_slice_in_dim(
+                full, going_down, (here + far) % ways * step, axis=dim
+            )
+    return full
 
 
 def interpolate(values, coords, strip_rows, tile_cols):
@@ -92,7 +108,7 @@
         "ack,nck->can",
         weighted,
         make_phasors(
-            lax.all_gather(station_rows, "stn", axis=0, tiled=True),
+            collect(station_rows, "stn", 0),
             lax.all_gather(iono_phase, "stn", axis=0, tiled=True),
             directions,
             freq_ratio,

time: 577 us -> 598 us (1.036)
  starting transfers between devices: 10.9 us -> 39.2 us
  blocking collectives: 45.8 us -> 23.8 us
  waiting for transfers between devices: 6.79 us -> 17.1 us
    ppermute x0 -> x15, starting transfers between devices: none -> 32 us  [the longest x7 30.9 us: collect(): lax.ppermute(going_down, axis, [(d, (d - 1) % ways) for d in range(ways)])]
    all_gather x1 -> x0, blocking collectives: 22 us -> none  [body(): lax.all_gather(station_rows, 'stn', axis=0, tiled=True)]
    ppermute x0 -> x15, waiting for transfers between devices: none -> 10.5 us  [the longest x8 10 us: collect(): lax.ppermute(going_up, axis, [(d, (d + 1) % ways) for d in range(ways)])]
  transfers between devices with their start and end apart: 2 -> 17, of which waited for: 1 -> 13; matrix products, arithmetic and copies ran while one was open for 1% -> 2% of each run, Pallas kernels for 0% -> 0%
where the time goes in v1:
time: 598 us; the launch traced here: 597 us
  local copies, waits for them, and re-layouts  433 us (72%)
  other arithmetic  75.2 us (13%)
  starting transfers between devices  39.2 us (7%)
  blocking collectives  23.8 us (4%)
  waiting for transfers between devices  17.1 us (3%)
  matrix products  8.91 us (1%)
    gather x2, local copies, waits for them, and re-layouts, interpolate(): lower_pair = (1.0 - frac_x) * values[corner] + frac_x * values[corner + 1]  181 us
    gather x1, local copies, waits for them, and re-layouts, interpolate(): values[corner + tile_cols + 1]  90.5 us
    gather x1, local copies, waits for them, and re-layouts, interpolate(): values[corner + tile_cols]  90.5 us
    another operation x1, other arithmetic  62.5 us
    scatter x1, local copies, waits for them, and re-layouts, body(): jnp.zeros((queries + 1,), jnp.float32).at[query_dest.reshape(-1)]  60.4 us
    ppermute x7, starting transfers between devices, collect(): lax.ppermute(going_down, axis, [(d, (d - 1) % ways) for d in range(ways)])  30.9 us
    all_gather x1, blocking collectives, body(): lax.all_gather(iono_phase, 'stn', axis=0, tiled=True)  19.4 us
  transfers between devices with their start and end apart: 17, of which 13 were waited for; matrix products, arithmetic and copies ran while one was open for 2% of the time, Pallas kernels for 0%

profile of v1, /device:TPU:0, one launch (start us, length us, event | category | flops | bytes accessed | tf_op | source)
XLA Modules:
  0.0 597.4 jit_solution(17344677377557127902)
XLA Ops:
  0.0 0.5 collective-permute-start
  0.5 5.0 collective-permute-start.1
  5.4 1.7 copy.13
  7.1 3.7 all-to-all-start
  10.8 0.8 slice_bitcast_fusion.2
  11.6 0.8 fusion.17
  12.4 0.9 copy.10
  13.4 0.7 fusion.19
  14.1 0.8 multiply_multiply_fusion
  14.9 0.1 multiply_add_fusion.3
  14.9 0.1 iota_compare_fusion
  15.2 2.1 copy.11
  17.4 0.8 dynamic_update_slice.48
  18.3 0.6 collective-permute-start.2
  18.8 4.0 collective-permute-start.3
  22.8 0.2 dynamic_update_slice.49
  23.0 0.2 dynamic_update_slice.50
  23.2 0.8 collective-permute-done.2
  24.0 0.1 collective-permute-done.3
  24.1 4.4 collective-permute-start.5
  28.5 0.2 dynamic_update_slice.51
  28.7 0.2 dynamic_update_slice.52
  28.9 0.8 collective-permute-done.4
  29.7 0.1 collective-permute-done.5
  29.8 4.4 collective-permute-start.7
  34.2 0.2 dynamic_update_slice.53
  34.4 0.2 dynamic_update_slice.54
  34.6 0.8 collective-permute-done.6
  35.4 0.1 collective-permute-done.7
  35.5 4.4 collective-permute-start.9
  39.9 0.2 dynamic_update_slice.55
  40.1 0.2 dynamic_update_slice.56
  40.3 0.8 collective-permute-done.8
  41.2 0.1 collective-permute-done.9
  41.2 4.4 collective-permute-start.11
  45.6 0.2 dynamic_update_slice.57
  45.8 0.2 dynamic_update_slice.58
  46.1 0.8 collective-permute-done.10
  46.9 0.1 collective-permute-done.11
  46.9 4.4 collective-permute-start.13
  51.3 0.2 dynamic_update_slice.59
  51.5 0.2 dynamic_update_slice.60
  51.8 0.8 collective-permute-done.12
  52.6 0.2 dynamic_update_slice.61
  52.8 0.3 dynamic_update_slice.62
  53.0 5.2 collective-permute-done.14
  58.4 0.3 compare_select_fusion.3
  58.7 0.2 compare_select_fusion.2
  58.9 90.5 %gather_fusion.1 = f32[16384]{0:T(1024)S(1)} fusion(f32[524288]{0:T(1024)S(1)} %bitcast.71, s32[16384]{0:T(1024)S(1)} %broadcast_clamp_fusion.2), kind=kCustom, calls=%fused_computation.1 | custom fusion | bytes 196608 | tf_op jit(solution)/shard_map/gather | solution.py:34
  149.5 90.5 %gather_fusion.2 = f32[16384]{0:T(1024)S(1)} fusion(f32[524288]{0:T(1024)S(1)} %bitcast.72, s32[16384]{0:T(1024)S(1)} %broadcast_clamp_fusion.1), kind=kCustom, calls=%fused_computation.2 | custom fusion | bytes 196608 | tf_op jit(solution)/shard_map/gather | solution.py:35
  240.0 90.5 %gather_fusion.3 = f32[16384]{0:T(1024)S(1)} fusion(f32[524288]{0:T(1024)S(1)} %bitcast.73, s32[16384]{0:T(1024)S(1)} %broadcast_clamp_fusion), kind=kCustom, calls=%fused_computation.3 | custom fusion | bytes 196608 | tf_op jit(solution)/shard_map/gather | solution.py:35
  330.6 90.5 %gather_fusion = f32[16384]{0:T(1024)S(1)} fusion(f32[524288]{0:T(1024)S(1)} %bitcast.74, s32[16384]{0:T(1024)S(1)} %broadcast_clamp_fusion.3), kind=kCustom, calls=%fused_computation | custom fusion | bytes 196608 | tf_op jit(solution)/shard_map/gather | solution.py:34
  421.2 1.0 multiply_add_fusion.2
  422.2 3.5 all-to-all-start.1
  425.7 0.2 multiply_add_fusion
  425.8 6.7 %all-to-all-done.1 = f32[16,1,1024]{2,1,0:T(1,128)S(1)} async-done(((f32[16,1,1024]{2,1,0:T(1,128)}), f32[16,1,1024]{2,1,0:T(1,128)S(1)}, u32[]{:S(2)}, u32[]{:S(2)}) %all-to-all-start.1) | async-done | bytes 65568 | tf_op jit(solution)/shard_map/all_to_all | solution.py:92
  432.5 60.4 %scatter_custom_fusion = f32[4097]{0:T(1024)S(1)} fusion(s32[16384]{0:T(1024)S(1)} %bitcast.86, f32[16384]{0:T(1024)S(1)} %bitcast.87, f32[]{:T(128)} %constant.114.clone.1), kind=kCustom, calls=%fused_computation.55 | custom fusion | bytes 16392 | tf_op jit(solution)/shard_map/scatter | solution.py:97
  492.9 4.4 all_gather.6
  497.3 19.4 %all_gather.7 = f32[256,512]{1,0:T(8,128)S(1)} all-gather(f32[16,512]{1,0:T(8,128)S(1)} %all_gather.6), channel_id=1, replica_groups=mesh['stn'=16,'chan'=2] {'stn'}, dimensions={0}, use_global_device_ids=true | all-gather | bytes 557056 | tf_op jit(solution)/shard_map/all_gather | solution.py:112
  516.7 4.2 multiply_convert_fusion.1
  520.9 3.9 fusion.16
  524.9 62.5 %cosine_convert_fusion = (bf16[256,32,512]{2,0,1:T(8,128)(2,1)}, bf16[256,32,512]{2,0,1:T(8,128)(2,1)}) fusion(f32[32]{0:T(128)S(1)} %copy-done, f32[256,512]{1,0:T(8,128)S(1)} %all_gather.7, f32[256,512]{1,0:T(8,128)S(1)} %multiply_add_fusion, f32[32]{0:T(128)S(1)} %get-tuple-element.24), kind=kLoop, calls=%fused_computation.11 | loop fusion | flops 20971520 | bytes 17826048 | tf_op jit(solution)/shard_map/convert
  587.4 8.9 %fusion = f32[32,32,256]{2,1,0:T(8,128)S(1)} fusion(bf16[256,32,512]{2,0,1:T(8,128)(2,1)} %get-tuple-element.8, bf16[256,32,512]{2,0,1:T(8,128)(2,1)} %get-tuple-element.7, bf16[16,32,512]{2,0,1:T(8,128)(2,1)S(1)} %fusion.16, bf16[16,32,512]{2,0,1:T(8,128)(2,1)S(1)} %get-tuple-element.10, bf16[16,32,512]{2,0,1:T(8,128)(2,1)S(1)} %get-tuple-element.9), kind=kOutput, calls=%fused_computation.6 | convolution fusion | flops 578813952 | bytes 19398656 | tf_op jit(solution)/shard_map/ack,nck->can/dot_general | solution.py:107
  596.3 1.1 broadcast_select_fusion
  (23 shorter events, 0.2 us)
Async XLA Ops:
  0.0 18.3 %collective-permute-start = (f32[16,3]{0,1:T(4,128)}, f32[16,3]{0,1:T(4,128)S(1)}, u32[]{:S(2)}, u32[]{:S(2)}) collective-permute-start(f32[16,3]{0,1:T(4,128)} %bitcast.94), channel_id=1, source_target_pairs={{0,2},{2,4},{4,6},{6,8},{8,10},{10,12},{12,14},{14,16},{16,18},{18... | collective-permute-start | bytes 584 | tf_op jit(solution)/shard_map/ppermute | solution.py:16
  0.5 18.3 %collective-permute-start.1 = (f32[16,3]{0,1:T(4,128)}, f32[16,3]{0,1:T(4,128)S(1)}, u32[]{:S(2)}, u32[]{:S(2)}) collective-permute-start(f32[16,3]{0,1:T(4,128)} %bitcast.95), channel_id=1, source_target_pairs={{0,30},{2,0},{4,2},{6,4},{8,6},{10,8},{12,10},{14,12},{16,14},{18,... | collective-permute-start | bytes 584 | tf_op jit(solution)/shard_map/ppermute | solution.py:19
  7.1 51.3 %all-to-all-start = ((f32[2,16,1024]{2,0,1:T(2,128)}), f32[2,16,1024]{2,0,1:T(2,128)S(1)}, u32[]{:S(2)}, u32[]{:S(2)}) async-start(f32[2,16,1024]{2,0,1:T(2,128)} %bitcast.70), calls=%async_computation | async-start | bytes 262144 | tf_op jit(solution)/shard_map/all_to_all | solution.py:88
  18.3 5.8 collective-permute-start.2
  18.8 5.3 collective-permute-start.3
  24.0 5.7 collective-permute-start.4
  24.1 5.7 collective-permute-start.5
  29.7 5.7 collective-permute-start.6
  29.8 5.7 collective-permute-start.7
  35.4 5.7 collective-permute-start.8
  35.5 5.7 collective-permute-start.9
  41.1 5.7 collective-permute-start.10
  41.2 5.7 collective-permute-start.11
  46.9 5.7 collective-permute-start.12
  46.9 5.8 collective-permute-start.13
  52.6 5.7 collective-permute-start.14
  330.6 186.1 %copy-start = (f32[32]{0:T(128)S(1)}, f32[32]{0:T(128)}, u32[]{:S(2)}) copy-start(f32[32]{0:T(128)} %param.13) | copy-start | bytes 388
  422.2 10.4 %all-to-all-start.1 = ((f32[16,1,1024]{2,1,0:T(1,128)}), f32[16,1,1024]{2,1,0:T(1,128)S(1)}, u32[]{:S(2)}, u32[]{:S(2)}) async-start(f32[16,1,1024]{2,1,0:T(1,128)} %multiply_add_fusion.2), calls=%async_computation.1 | async-start | bytes 131072 | tf_op jit(solution)/shard_map/all_to_all | solution.py:92
